TPU v7x, 512 devices: a whole 4x4x16 slice. The times are simulated.
512 devices in a mesh: rows: 64 (over x, z), batch: 8 (over y, core).
Axes of the slice: x: 4, y: 4, z: 16, core: 2. Of those that a mesh axis runs over, the one named last changes fastest.
Arguments:
- frames: bfloat16 [16384, 4096], P('rows', 'batch'), may hold values from -40 to 40
- tap_table: int32 [63], replicated, may hold values from -128 to 127
- sketch_matrix: bfloat16 [512, 256], replicated, may hold values from -0.25 to 0.25
- decay_rates: float32 [8, 256], P('batch'), may hold values from 0.5 to 1
Outputs:
- basis: float32 [8, 16384, 256], P('batch', 'rows')
- factor: float32 [8, 256, 256], P('batch')
- coeffs: float32 [8, 256, 512], P('batch')
All inputs are finite; a program needn't handle non-finite values.
Results may differ from a plain program's by a relative error of at most 0.0039.
The roundings to bfloat16 on the way count: a program that leaves them out, or rounds other values in their place, can miss the bound.
Values may be sent and summed in bfloat16 or wider, within the bound.
No kernel may reach another device: no remote copies, remote signals or barrier semaphores. Data moves between devices by JAX's collectives and lax.ppermute only.
A program may use at most 64 MiB of HBM per device.

v0:
```python
import math
import jax
import jax.numpy as jnp
from jax import lax
from jax.sharding import PartitionSpec as P

HIGH = lax.Precision.HIGHEST


def passed_along(x, axis, by):
    length = lax.axis_size(axis)
    pairs = [(i, i + by) for i in range(length) if 0 <= i + by < length]
    return lax.ppermute(x, axis, pairs)


def band_matrix(coefs, rows_count, cols_count, offset):
    row_ids = lax.broadcasted_iota(jnp.int32, (rows_count, cols_count), 0)
    col_ids = lax.broadcasted_iota(jnp.int32, (rows_count, cols_count), 1)
    lag_ids = col_ids - row_ids + offset
    valid = (lag_ids >= 0) & (lag_ids < coefs.shape[0])
    values = jnp.take(coefs, jnp.clip(lag_ids, 0, coefs.shape[0] - 1))
    return jnp.where(valid, values, jnp.zeros_like(values))


def gram_of(block):
    return lax.dot_general(
        block, block, (((0,), (0,)), ((), ())), precision=HIGH, preferred_element_type=jnp.float32
    )


def cross_of(left, right):
    return lax.dot_general(
        left, right, (((0,), (0,)), ((), ())), precision=HIGH, preferred_element_type=jnp.float32
    )


def shards(frames, tap_table, sketch_matrix, decay_rates):
    rows_here, frame_count = frames.shape
    tap_count = tap_table.shape[0]
    npoints = rows_here * lax.axis_size("rows")
    batch_count = lax.axis_size("batch")
    coefs = (tap_table.astype(jnp.float32) / 1024.0).astype(jnp.bfloat16)
    main_band = band_matrix(coefs, frame_count, frame_count, 0)
    hist_band = band_matrix(coefs, tap_count - 1, frame_count, tap_count - 1)
    history = passed_along(frames[:, frame_count - (tap_count - 1) :], "batch", 1)
    filtered = (
        jnp.dot(frames, main_band, preferred_element_type=jnp.float32)
        + jnp.dot(history, hist_band, preferred_element_type=jnp.float32)
    ).astype(jnp.bfloat16)
    sketched = jnp.dot(filtered, sketch_matrix, preferred_element_type=jnp.float32)
    rates = decay_rates[0]

    def one_turn(turn_index, carried):
        return rates[None, :] * passed_along(carried, "batch", 1) + sketched

    weighted = lax.fori_loop(0, batch_count - 1, one_turn, sketched)
    root_points = math.sqrt(npoints)
    rank_count = weighted.shape[1]
    filtered_wide = filtered.astype(jnp.float32)
    lower_one = jnp.linalg.cholesky(lax.psum(gram_of(weighted), "rows"))
    final_q = lax.linalg.triangular_solve(
        lower_one, weighted, left_side=False, lower=True, transpose_a=True
    )
    scaled = final_q * root_points
    partial_proj = cross_of(scaled, filtered_wide)
    projected = lax.psum(partial_proj, "rows") * (math.sqrt(rank_count) / npoints)
    upper = lower_one.T / root_points
    return (scaled[None], upper[None], projected[None])


def solution(mesh):
    placed = (P("rows", "batch"), P(), P(), P("batch", None))
    return jax.shard_map(
        shards,
        mesh=mesh,
        in_specs=placed,
        out_specs=(P("batch", "rows", None), P("batch", None, None), P("batch", None, None)),
        check_vma=False,
    )
```

profile of v0, /device:TPU:8, one launch (start us, length us, event | category | flops | bytes accessed | tf_op | source)
XLA Modules:
  0.0 904.6 jit_solution(605645552439976620)
XLA Ops:
  7.2 0.0 copy-start
  7.2 0.0 copy-start.4
  7.2 0.0 all-reduce.4.cloned.1.call-start
  7.2 0.9 slice.45
  8.2 1.9 collective-permute-start.1
  10.1 0.0 copy-done.4
  10.1 0.7 fusion.427
  10.9 0.7 fusion.428
  11.5 0.7 fusion.425
  12.3 0.7 fusion.426
  13.0 0.0 copy-start.3
  13.0 0.9 copy-done.3
  14.0 41.2 %fusion.190 = f32[512,256]{1,0:T(8,128)S(1)} fusion(bf16[256,512]{1,0:T(8,128)(2,1)S(1)} %copy-done.3, bf16[]{:T(256)} %bitcast.113, bf16[]{:T(256)} %bitcast.114, bf16[]{:T(256)} %bitcast.115, bf16[]{:T(256)} %bitcast.116, bf16[]{:T(256)} %bitcast.117, bf16[]{:T(256)} %bitcast.119, bf16[]{:T(256)} %bitcast.118, bf16[]{:T(256)} %bitcast.2, bf16[]{:T(256)} %bitcast.4, ...), kind=kOutput, calls=%fused_computation.200 | convolution fusion | flops 171442176 | bytes 786558 | tf_op jit(solution)/shard_map/dot_general | solution.py:47
  55.2 185.6 %gather_fusion = bf16[31744]{0:T(1024)(128)(2,1)S(1)} fusion(bf16[63]{0:T(256)(128)(2,1)S(1)} %multiply_convert_fusion, s32[31744]{0:T(1024)S(1)} %broadcast_clamp_fusion), kind=kCustom, calls=%fused_computation | custom fusion | bytes 253952 | tf_op jit(solution)/shard_map/jit(_take)/gather | solution.py:21
  240.9 0.0 collective-permute-done.1
  240.9 0.3 fusion
  241.2 0.0 copy-done
  241.2 0.3 fusion.429
  241.5 0.0 copy-start.2
  241.5 0.6 copy-done.2
  242.1 54.2 %while.11 = (s32[]{:T(128)}, f32[256,256]{1,0:T(8,128)S(1)}, f32[1,256]{1,0:T(1,128)S(1)}, f32[256,256]{1,0:T(8,128)S(1)}, s32[]{:T(128)}) while((s32[]{:T(128)}, f32[256,256]{1,0:T(8,128)S(1)}, f32[1,256]{1,0:T(1,128)S(1)}, f32[256,256]{1,0:T(8,128)S(1)}, s32[]{:T(128)}) %tuple.112), condition=%wide.region_1.2_spmd, body=%wide.region_0.1_spmd.sunk | while | flops 131074 | bytes 1836133 | solution.py:56
  242.1 3.6 collective-permute-start
  245.7 4.1 collective-permute-done
  249.9 1.9 collective-permute-start
  251.8 5.8 collective-permute-done
  257.6 1.9 collective-permute-start
  259.6 5.8 collective-permute-done
  265.4 1.9 collective-permute-start
  267.3 5.8 collective-permute-done
  273.1 1.9 collective-permute-start
  275.0 5.8 collective-permute-done
  280.8 1.9 collective-permute-start
  282.8 5.8 collective-permute-done
  288.6 1.9 collective-permute-start
  290.5 5.8 collective-permute-done
  296.3 1.3 fusion.430
  297.6 0.0 all-reduce.4.cloned.1.call-update
  297.7 0.2 all-reduce.6.cloned.1.call-start
  297.9 271.0 %all-reduce.4.cloned.1.call-done = f32[256,256]{0,1:T(8,128)} async-done(((f32[256,256]{0,1:T(8,128)}), f32[256,256]{0,1:T(8,128)}) %all-reduce.4.cloned.1.call-update) | async-done | bytes 262160 | tf_op jit(solution)/shard_map/psum | solution.py:60
  568.9 0.0 copy-start.1
  568.9 1.1 copy.12
  570.1 0.0 copy-done.1
  570.2 11.7 %cholesky.50 = f32[128,128]{1,0:T(8,128)S(1)} custom-call(f32[128,128]{1,0:T(8,128)S(1)} %cholesky.118), custom_call_target="Cholesky" | custom-call | tf_op jit(solution)/shard_map/jit(cholesky)/cholesky | solution.py:60
  581.9 9.8 %custom-call.14 = f32[1,128,128]{1,2,0:T(8,128)S(1)} custom-call(f32[1,128,128]{2,1,0:T(8,128)S(1)} %get-tuple-element.63), custom_call_target="InvertDiagBlocksLowerTriangular" | custom-call | tf_op jit(solution)/shard_map/jit(cholesky)/cholesky | solution.py:60
  591.8 0.2 constant_dynamic-update-slice_fusion.1
  592.0 0.3 convolution_subtract_fusion.1
  592.2 11.7 %cholesky.105 = f32[128,128]{1,0:T(8,128)S(1)} custom-call(f32[128,128]{1,0:T(8,128)S(1)} %convolution_subtract_fusion.1), custom_call_target="Cholesky" | custom-call | tf_op jit(solution)/shard_map/jit(cholesky)/cholesky | solution.py:60
  604.0 0.6 compare_reduce_fusion
  606.0 0.1 triangular_solve.64
  606.0 4.2 while.12
  606.2 0.6 fusion.443
  606.8 1.4 bitcast_dynamic-update-slice_fusion.2
  608.2 0.6 fusion.443
  608.8 1.4 bitcast_dynamic-update-slice_fusion.2
  610.2 19.7 %custom-call.15 = f32[2,128,128]{1,2,0:T(8,128)S(1)} custom-call(f32[2,128,128]{2,1,0:T(8,128)S(1)} %get-tuple-element.33), custom_call_target="InvertDiagBlocksLowerTriangular" | custom-call | tf_op jit(solution)/shard_map/triangular_solve | solution.py:61
  629.9 0.3 fusion.330
  630.2 0.4 convolution_subtract_fusion
  630.6 0.3 fusion.341
  630.9 1.2 fusion.259
  632.1 0.0 all-reduce.6.cloned.1.call-update
  632.2 0.8 copy.13
  633.0 0.8 copy.14
  633.9 262.0 %all-reduce.6.cloned.1.call-done = f32[256,512]{1,0:T(8,128)} async-done(((f32[256,512]{1,0:T(8,128)}), f32[256,512]{1,0:T(8,128)}) %all-reduce.6.cloned.1.call-update) | async-done | bytes 524304 | tf_op jit(solution)/shard_map/psum | solution.py:66
  895.9 1.9 multiply_bitcast_fusion
  (24 shorter events, 0.6 us)
Async XLA Ops:
  7.2 234.0 %copy-start = (bf16[512,256]{1,0:T(8,128)(2,1)S(1)}, bf16[512,256]{1,0:T(8,128)(2,1)}, u32[]{:S(2)}) copy-start(bf16[512,256]{1,0:T(8,128)(2,1)} %param.8) | copy-start | bytes 786436
  7.2 2.9 copy-start.4
  7.2 561.7 %all-reduce.4.cloned.1.call-start = ((), (), s32[]{:S(2)}) async-start(), calls=%async_computation | async-start | bytes 524288 | tf_op jit(solution)/shard_map/psum | solution.py:60
  8.2 232.7 %collective-permute-start.1 = (bf16[256,62]{1,0:T(8,128)(2,1)S(1)}, bf16[256,62]{1,0:T(8,128)(2,1)S(1)}, u32[]{:S(2)}, u32[]{:S(2)}) collective-permute-start(bf16[256,62]{1,0:T(8,128)(2,1)S(1)} %slice.45), channel_id=1, source_target_pairs={{0,1},{1,2},{2,3},{3,4},{4,5},{5,6},{6,7},{8,9},{9,10},{10,11},{11... | collective-permute-start | bytes 95240 | tf_op jit(solution)/shard_map/ppermute | solution.py:13
  13.0 1.0 copy-start.3
  241.5 0.7 copy-start.2
  242.1 7.7 collective-permute-start
  249.9 7.7 collective-permute-start
  257.6 7.7 collective-permute-start
  265.4 7.7 collective-permute-start
  273.1 7.7 collective-permute-start
  280.8 7.7 collective-permute-start
  288.6 7.7 collective-permute-start
  297.7 598.3 %all-reduce.6.cloned.1.call-start = ((), (), s32[]{:S(2)}) async-start(), calls=%async_computation.1 | async-start | bytes 1048576 | tf_op jit(solution)/shard_map/psum | solution.py:66
  568.9 1.2 copy-start.1
Sparse Core Ops, SparseCore 0:
  297.8 271.1 all-reduce.3
  632.3 263.5 all-reduce.5
where the time goes:
time: 906 us; the launch traced here: 905 us
  waiting for transfers between devices  572 us (63%)
  local copies, waits for them, and re-layouts  198 us (22%)
  other arithmetic  55.9 us (6%)
  matrix products  45.7 us (5%)
  starting transfers between devices  17.3 us (2%)
  between operations  15.6 us (2%)
    psum x1, waiting for transfers between devices, shards(): lower_one = jnp.linalg.cholesky(lax.psum(gram_of(weighted), 'rows'))  271 us
    psum x1, waiting for transfers between devices, shards(): lax.psum(partial_proj, 'rows') * (math.sqrt(rank_count) / npoints)  262 us
    gather x6, local copies, waits for them, and re-layouts, band_matrix(): values = jnp.take(coefs, jnp.clip(lag_ids, 0, coefs.shape[0] - 1))  189 us
    dot_general x1, matrix products, shards(): jnp.dot(frames, main_band, preferred_element_type=jnp.float32)  41.2 us
    ppermute x8, waiting for transfers between devices, passed_along(): return lax.ppermute(x, axis, pairs)  38.7 us
    another operation x6, other arithmetic, shards(): lower_one = jnp.linalg.cholesky(lax.psum(gram_of(weighted), 'rows'))  33.9 us
    another operation x2, other arithmetic, shards(): lax.linalg.triangular_solve(lower_one, weighted, left_side=False, lower=T...  19.7 us
  transfers between devices with their start and end apart: 10, of which 9 were waited for; matrix products, arithmetic and copies ran while one was open for 26% of the time, Pallas kernels for 0%

commit v1 on v0

--- a/solution.py
+++ b/solution.py
@@ -57,7 +57,7 @@
     root_points = math.sqrt(npoints)
     rank_count = weighted.shape[1]
     filtered_wide = filtered.astype(jnp.float32)
-    lower_one = jnp.linalg.cholesky(lax.psum(gram_of(weighted), "rows"))
+    lower_one = jnp.linalg.cholesky(jnp.sum(lax.all_gather(gram_of(weighted), "rows"), axis=0))
     final_q = lax.linalg.triangular_solve(
         lower_one, weighted, left_side=False, lower=True, transpose_a=True
     )

time: 906 us -> 840 us (0.927)
  waiting for transfers between devices: 572 us -> 500 us
    psum x1 -> x0, waiting for transfers between devices: 271 us -> none  [shards(): lower_one = jnp.linalg.cholesky(lax.psum(gram_of(weighted), 'rows'))]
    all_gather x0 -> x1, waiting for transfers between devices: none -> 197 us  [shards(): lax.all_gather(gram_of(weighted), 'rows')]
  transfers between devices with their start and end apart: 10 -> 10, of which waited for: 9 -> 9; matrix products, arithmetic and copies ran while one was open for 26% -> 28% of each run, Pallas kernels for 0% -> 0%
where the time goes in v1:
time: 840 us; the launch traced here: 839 us
  waiting for transfers between devices  500 us (60%)
  local copies, waits for them, and re-layouts  195 us (23%)
  other arithmetic  63.4 us (8%)
  matrix products  46.7 us (6%)
  starting transfers between devices  17.3 us (2%)
  between operations  15.6 us (2%)
    psum x1, waiting for transfers between devices, shards(): lax.psum(partial_proj, 'rows') * (math.sqrt(rank_count) / npoints)  264 us
    all_gather x1, waiting for transfers between devices, shards(): lax.all_gather(gram_of(weighted), 'rows')  197 us
    gather x6, local copies, waits for them, and re-layouts, band_matrix(): values = jnp.take(coefs, jnp.clip(lag_ids, 0, coefs.shape[0] - 1))  189 us
    dot_general x1, matrix products, shards(): jnp.dot(frames, main_band, preferred_element_type=jnp.float32)  42.2 us
    ppermute x8, waiting for transfers between devices, passed_along(): return lax.ppermute(x, axis, pairs)  38.7 us
    another operation x6, other arithmetic, shards(): jnp.linalg.cholesky(jnp.sum(lax.all_gather(gram_of(weighted), 'rows'), ax...  33.9 us
    another operation x2, other arithmetic, shards(): lax.linalg.triangular_solve(lower_one, weighted, left_side=False, lower=T...  19.7 us
    ppermute x8, starting transfers between devices, passed_along(): return lax.ppermute(x, axis, pairs)  17 us
  transfers between devices with their start and end apart: 10, of which 9 were waited for; matrix products, arithmetic and copies ran while one was open for 28% of the time, Pallas kernels for 0%

profile of v1, /device:TPU:8, one launch (start us, length us, event | category | flops | bytes accessed | tf_op | source)
XLA Modules:
  0.0 838.7 jit_solution(3450860081276768745)
XLA Ops:
  7.2 0.0 copy-start
  7.2 0.0 all-gather.3.cloned.1.call-start
  7.2 1.0 slice.45
  8.2 1.9 collective-permute-start.1
  10.1 0.7 multiply_convert_fusion
  10.8 0.7 fusion.425
  11.5 0.7 fusion.427
  12.2 0.7 fusion.426
  13.0 0.7 fusion.428
  13.7 42.2 %fusion.190 = f32[512,256]{1,0:T(8,128)S(1)} fusion(bf16[256,512]{1,0:T(8,128)(2,1)} %param.6, bf16[]{:T(256)} %bitcast.113, bf16[]{:T(256)} %bitcast.114, bf16[]{:T(256)} %bitcast.115, bf16[]{:T(256)} %bitcast.116, bf16[]{:T(256)} %bitcast.117, bf16[]{:T(256)} %bitcast.119, bf16[]{:T(256)} %bitcast.118, bf16[]{:T(256)} %bitcast.2, bf16[]{:T(256)} %bitcast.4, ...), kind=kOutput, calls=%fused_computation.200 | convolution fusion | flops 171442176 | bytes 786558 | tf_op jit(solution)/shard_map/dot_general | solution.py:47
  56.0 0.0 copy-start.1
  56.0 185.6 %gather_fusion = bf16[31744]{0:T(1024)(128)(2,1)S(1)} fusion(bf16[63]{0:T(256)(128)(2,1)S(1)} %multiply_convert_fusion, s32[31744]{0:T(1024)S(1)} %broadcast_clamp_fusion), kind=kCustom, calls=%fused_computation | custom fusion | bytes 253952 | tf_op jit(solution)/shard_map/jit(_take)/gather | solution.py:21
  241.7 0.0 collective-permute-done.1
  241.7 0.3 fusion
  241.9 0.0 copy-done
  241.9 0.3 fusion.429
  242.2 0.0 copy-done.1
  242.2 54.2 %while.11 = (s32[]{:T(128)}, f32[256,256]{1,0:T(8,128)S(1)}, f32[1,256]{1,0:T(1,128)S(1)}, f32[256,256]{1,0:T(8,128)S(1)}, s32[]{:T(128)}) while((s32[]{:T(128)}, f32[256,256]{1,0:T(8,128)S(1)}, f32[1,256]{1,0:T(1,128)S(1)}, f32[256,256]{1,0:T(8,128)S(1)}, s32[]{:T(128)}) %tuple.113), condition=%wide.region_1.2_spmd, body=%wide.region_0.1_spmd.sunk | while | flops 131074 | bytes 1836133 | solution.py:56
  242.2 3.6 collective-permute-start
  245.8 4.1 collective-permute-done
  250.0 1.9 collective-permute-start
  251.9 5.8 collective-permute-done
  257.7 1.9 collective-permute-start
  259.7 5.8 collective-permute-done
  265.5 1.9 collective-permute-start
  267.4 5.8 collective-permute-done
  273.2 1.9 collective-permute-start
  275.1 5.8 collective-permute-done
  281.0 1.9 collective-permute-start
  282.9 5.8 collective-permute-done
  288.7 1.9 collective-permute-start
  290.6 5.8 collective-permute-done
  296.4 1.3 fusion.430
  297.7 0.0 all-gather.3.cloned.1.call-update
  297.8 0.2 all-reduce.3.cloned.1.call-start
  298.0 197.1 %all-gather.3.cloned.1.call-done = f32[16384,256]{1,0:T(8,128)} async-done(((f32[256,256]{1,0:T(8,128)}), f32[16384,256]{1,0:T(8,128)}) %all-gather.3.cloned.1.call-update) | async-done | bytes 16777232 | tf_op jit(solution)/shard_map/all_gather | solution.py:60
  495.1 6.8 reduce_sum.9
  502.0 0.1 copy.13
  502.2 11.7 %cholesky.50 = f32[128,128]{1,0:T(8,128)S(1)} custom-call(f32[128,128]{1,0:T(8,128)S(1)} %cholesky.118), custom_call_target="Cholesky" | custom-call | tf_op jit(solution)/shard_map/jit(cholesky)/cholesky | solution.py:60
  513.9 9.8 %custom-call.14 = f32[1,128,128]{1,2,0:T(8,128)S(1)} custom-call(f32[1,128,128]{2,1,0:T(8,128)S(1)} %get-tuple-element.66), custom_call_target="InvertDiagBlocksLowerTriangular" | custom-call | tf_op jit(solution)/shard_map/jit(cholesky)/cholesky | solution.py:60
  523.7 0.2 constant_dynamic-update-slice_fusion.1
  524.0 0.3 convolution_subtract_fusion.1
  524.2 11.7 %cholesky.105 = f32[128,128]{1,0:T(8,128)S(1)} custom-call(f32[128,128]{1,0:T(8,128)S(1)} %convolution_subtract_fusion.1), custom_call_target="Cholesky" | custom-call | tf_op jit(solution)/shard_map/jit(cholesky)/cholesky | solution.py:60
  536.0 0.6 compare_reduce_fusion
  538.0 0.1 triangular_solve.64
  538.0 4.2 while.12
  538.2 0.6 fusion.443
  538.8 1.4 bitcast_dynamic-update-slice_fusion.2
  540.2 0.6 fusion.443
  540.8 1.4 bitcast_dynamic-update-slice_fusion.2
  542.2 19.7 %custom-call.15 = f32[2,128,128]{1,2,0:T(8,128)S(1)} custom-call(f32[2,128,128]{2,1,0:T(8,128)S(1)} %get-tuple-element.33), custom_call_target="InvertDiagBlocksLowerTriangular" | custom-call | tf_op jit(solution)/shard_map/triangular_solve | solution.py:61
  561.9 0.3 fusion.330
  562.2 0.4 convolution_subtract_fusion
  562.6 0.3 fusion.341
  562.9 1.2 fusion.259
  564.1 0.0 all-reduce.3.cloned.1.call-update
  564.2 0.8 copy.14
  565.0 0.8 copy.15
  565.9 264.2 %all-reduce.3.cloned.1.call-done = f32[256,512]{1,0:T(8,128)} async-done(((f32[256,512]{1,0:T(8,128)}), f32[256,512]{1,0:T(8,128)}) %all-reduce.3.cloned.1.call-update) | async-done | bytes 524304 | tf_op jit(solution)/shard_map/psum | solution.py:66
  830.0 1.9 multiply_bitcast_fusion
  (23 shorter events, 0.6 us)
Async XLA Ops:
  7.2 234.8 %copy-start = (bf16[512,256]{1,0:T(8,128)(2,1)S(1)}, bf16[512,256]{1,0:T(8,128)(2,1)}, u32[]{:S(2)}) copy-start(bf16[512,256]{1,0:T(8,128)(2,1)} %param.8) | copy-start | bytes 786436
  7.2 487.9 %all-gather.3.cloned.1.call-start = ((), (), s32[]{:S(2)}) async-start(), calls=%async_computation.1 | async-start | bytes 17039360 | tf_op jit(solution)/shard_map/all_gather | solution.py:60
  8.2 233.5 %collective-permute-start.1 = (bf16[256,62]{1,0:T(8,128)(2,1)S(1)}, bf16[256,62]{1,0:T(8,128)(2,1)S(1)}, u32[]{:S(2)}, u32[]{:S(2)}) collective-permute-start(bf16[256,62]{1,0:T(8,128)(2,1)S(1)} %slice.45), channel_id=1, source_target_pairs={{0,1},{1,2},{2,3},{3,4},{4,5},{5,6},{6,7},{8,9},{9,10},{10,11},{11... | collective-permute-start | bytes 95240 | tf_op jit(solution)/shard_map/ppermute | solution.py:13
  56.0 186.3 %copy-start.1 = (f32[1,256]{1,0:T(1,128)S(1)}, f32[1,256]{1,0:T(1,128)}, u32[]{:S(2)}) copy-start(f32[1,256]{1,0:T(1,128)} %param.9) | copy-start | bytes 3076
  242.2 7.7 collective-permute-start
  250.0 7.7 collective-permute-start
  257.7 7.7 collective-permute-start
  265.5 7.7 collective-permute-start
  273.2 7.7 collective-permute-start
  281.0 7.7 collective-permute-start
  288.7 7.7 collective-permute-start
  297.8 532.3 %all-reduce.3.cloned.1.call-start = ((), (), s32[]{:S(2)}) async-start(), calls=%async_computation | async-start | bytes 1048576 | tf_op jit(solution)/shard_map/psum | solution.py:66
Sparse Core Ops, SparseCore 0:
  297.9 197.1 all-gather.2
  564.3 265.6 all-reduce.2
